TPU v7x, 256 devices: a whole 4x4x8 slice. The times are simulated.
256 devices in a mesh: aa: 32 (over z, x), ba: 8 (over y, core).
Axes of the slice: x: 4, y: 4, z: 8, core: 2. Of those that a mesh axis runs over, the one named last changes fastest.
Arguments:
- snapshots: float32 [8192, 65536], P(('aa', 'ba')), may hold values from -125 to 125
Outputs:
- factors: float32 [8, 64, 64], replicated
- pod_modes: float32 [8, 64, 65536], P(None, None, ('aa', 'ba'))
All inputs are finite; a program needn't handle non-finite values.
Results may differ from a plain program's by a relative error of at most 0.000098.
Values sent between devices are 32-bit elements; how exact they have to be, the bound alone decides.
No kernel may reach another device: no remote copies, remote signals or barrier semaphores. Data moves between devices by JAX's collectives and lax.ppermute only.
A program may use at most 128 MiB of HBM per device.

v0:
```python
import math
import jax
import jax.numpy as jnp
from jax import lax
from jax.sharding import PartitionSpec as P

FREQS = 8


def spectral_rows(block_len, points, first, count):
    sample = first + jnp.arange(count, dtype=jnp.int32)
    harmonic = jnp.arange(1, FREQS + 1, dtype=jnp.int32)
    phase_turns = (sample[:, None] * harmonic[None, :] % block_len).astype(jnp.float32) * (
        2.0 * math.pi / block_len
    )
    full = jnp.arange(block_len, dtype=jnp.int32).astype(jnp.float32) * (2.0 * math.pi / block_len)
    full_window = 0.5 - 0.5 * jnp.cos(full)
    norm_scale = 1.0 / jnp.sqrt(points * jnp.sum(full_window * full_window))
    sample_angle = sample.astype(jnp.float32) * (2.0 * math.pi / block_len)
    window = 0.5 - 0.5 * jnp.cos(sample_angle)
    cosine = window[:, None] * jnp.cos(phase_turns) * norm_scale
    sine = -window[:, None] * jnp.sin(phase_turns) * norm_scale
    return jnp.stack([cosine, sine], axis=1)


def local(snapshots):
    time_dev, points = snapshots.shape
    n_aa = lax.axis_size("aa")
    n_ba = lax.axis_size("ba")
    pts_dev = points // (n_aa * n_ba)
    block_len = time_dev * n_ba
    u = lax.axis_index("ba")
    table = spectral_rows(block_len, points, u * time_dev, time_dev)
    arranged = snapshots.reshape(time_dev, n_aa, n_ba, pts_dev)
    partial = jnp.einsum("savq,sgf->vgfaq", arranged, table, precision=lax.Precision.HIGHEST)
    block_spec = lax.psum_scatter(partial, "ba", scatter_dimension=0, tiled=True)
    spectra = lax.all_to_all(block_spec, "aa", split_axis=3, concat_axis=0, tiled=True)
    blocks = spectra.shape[0]
    columns = 2 * blocks
    cols = jnp.transpose(spectra.reshape(blocks, 2, FREQS, pts_dev), (2, 0, 1, 3)).reshape(
        FREQS, columns, pts_dev
    )
    product = jnp.einsum("fip,fjp->fij", cols, cols, precision=lax.Precision.HIGHEST)
    gram_sum = lax.psum(product, ("aa", "ba"))
    lower_factor = jnp.linalg.cholesky(gram_sum)
    identity = jnp.broadcast_to(jnp.eye(columns, dtype=gram_sum.dtype), lower_factor.shape)
    inverse = lax.linalg.triangular_solve(lower_factor, identity, left_side=True, lower=True)
    pod_modes = math.sqrt(points) * jnp.einsum(
        "fij,fjp->fip", inverse, cols, precision=lax.Precision.HIGHEST
    )
    return (jnp.swapaxes(lower_factor, 1, 2), pod_modes)


def solution(mesh):
    placed = (P(("aa", "ba"), None),)
    return jax.shard_map(
        local,
        mesh=mesh,
        in_specs=placed,
        out_specs=(P(), P(None, None, ("aa", "ba"))),
        check_vma=False,
    )
```

profile of v0, /device:TPU:2, one launch (start us, length us, event | category | flops | bytes accessed | tf_op | source)
XLA Modules:
  0.0 479.1 jit_solution(12910174082356562652)
XLA Ops:
  7.2 0.0 all-reduce.6.cloned.1.call-start
  7.3 0.6 multiply_reduce_fusion
  8.6 5.9 %copy.38 = f32[4,8,256,256]{3,2,1,0:T(8,128)S(1)} copy(f32[4,8,256,256]{3,1,2,0:T(8,128)} %bitcast.42) | data formatting | bytes 16777216
  14.6 0.1 multiply_multiply_fusion.1
  14.7 0.0 copy-start
  14.7 9.2 %fusion.3 = f32[8,2,8,32,256]{4,2,0,3,1:T(8,128)} fusion(f32[32,32,8,256]{3,2,1,0:T(8,128)S(1)} %bitcast.41, f32[32,1,8]{0,2,1:T(8,128)S(1)} %get-tuple-element.13, f32[32,1,8]{0,2,1:T(8,128)S(1)} %get-tuple-element.12), kind=kOutput, calls=%fused_computation.3 | convolution fusion | flops 402653696 | bytes 12584960 | tf_op jit(solution)/shard_map/savq,sgf->vgfaq/dot_general | solution.py:35
  23.9 0.0 all-reduce.6.cloned.1.call-update
  23.9 0.0 copy-done
  23.9 0.6 dynamic-slice
  24.5 80.1 %all-reduce.6.cloned.1.call-done = f32[8,2,8,32,256]{4,2,0,3,1:T(8,128)} async-done(((f32[8,2,8,32,256]{4,2,0,3,1:T(8,128)}), f32[8,2,8,32,256]{4,2,0,3,1:T(8,128)}) %all-reduce.6.cloned.1.call-update) | async-done | bytes 4194320
  104.6 1.7 constant_dynamic-slice_fusion
  106.3 0.9 copy.25
  107.2 10.1 %all-to-all-start = ((f32[1,2,8,32,256]{4,2,0,1,3:T(8,128)}), f32[1,2,8,32,256]{4,2,0,1,3:T(8,128)S(1)}, u32[]{:S(2)}, u32[]{:S(2)}) async-start(f32[1,2,8,32,256]{4,2,0,1,3:T(8,128)} %copy.25), calls=%async_computation | async-start | bytes 1048576 | tf_op jit(solution)/shard_map/all_to_all | solution.py:37
  117.3 0.2 all-reduce.4.cloned.1.call-start
  117.6 14.8 %all-to-all-done = f32[1,2,8,32,256]{4,2,0,1,3:T(8,128)S(1)} async-done(((f32[1,2,8,32,256]{4,2,0,1,3:T(8,128)}), f32[1,2,8,32,256]{4,2,0,1,3:T(8,128)S(1)}, u32[]{:S(2)}, u32[]{:S(2)}) %all-to-all-start) | async-done | bytes 524320 | tf_op jit(solution)/shard_map/all_to_all | solution.py:37
  132.4 1.6 fusion.7
  134.0 0.0 all-reduce.4.cloned.1.call-update
  134.0 246.7 %all-reduce.4.cloned.1.call-done = f32[8,64,64]{1,2,0:T(8,128)} async-done(((f32[8,64,64]{1,2,0:T(8,128)}), f32[8,64,64]{1,2,0:T(8,128)}) %all-reduce.4.cloned.1.call-update) | async-done | bytes 131088 | tf_op jit(solution)/shard_map/psum | solution.py:44
  380.7 1.1 copy.29
  381.8 1.0 fusion.11
  382.8 46.9 %custom-call.7 = f32[8,64,64]{2,1,0:T(8,128)S(1)} custom-call(f32[8,64,64]{2,1,0:T(8,128)S(1)} %fusion.11), custom_call_target="Cholesky" | custom-call | tf_op jit(solution)/shard_map/jit(cholesky)/cholesky | solution.py:45
  429.8 0.1 compare_reduce_fusion
  429.9 0.1 select_bitcast_fusion
  430.0 39.3 %custom-call.8 = f32[8,1,64,64]{2,3,1,0:T(8,128)S(1)} custom-call(f32[8,1,64,64]{3,2,1,0:T(8,128)S(1)} %get-tuple-element.10), custom_call_target="InvertDiagBlocksLowerTriangular" | custom-call | tf_op jit(solution)/shard_map/triangular_solve | solution.py:47
  469.3 0.6 fusion.9
  469.9 1.5 convolution_multiply_fusion
  471.5 0.8 copy.32
  (7 shorter events, 0.1 us)
Async XLA Ops:
  7.2 97.5 %all-reduce.6.cloned.1.call-start = ((), (), s32[]{:S(2)}) async-start(), calls=%async_computation.2 | async-start | bytes 8388608
  14.7 9.2 %copy-start = (u32[256]{0:T(256)S(1)}, u32[256]{0:T(256)}, u32[]{:S(2)}) copy-start(u32[256]{0:T(256)} %constant.81) | copy-start | bytes 3076
  107.2 25.2 %all-to-all-start = ((f32[1,2,8,32,256]{4,2,0,1,3:T(8,128)}), f32[1,2,8,32,256]{4,2,0,1,3:T(8,128)S(1)}, u32[]{:S(2)}, u32[]{:S(2)}) async-start(f32[1,2,8,32,256]{4,2,0,1,3:T(8,128)} %copy.25), calls=%async_computation | async-start | bytes 1048576 | tf_op jit(solution)/shard_map/all_to_all | solution.py:37
  117.3 263.4 %all-reduce.4.cloned.1.call-start = ((), (), s32[]{:S(2)}) async-start(), calls=%async_computation.1 | async-start | bytes 524288 | tf_op jit(solution)/shard_map/psum | solution.py:44
Sparse Core Ops, SparseCore 0:
  24.0 80.5 all-reduce.5
  134.1 246.5 all-reduce.3
where the time goes:
time: 479 us
  waiting for transfers between devices  342 us (71%)
  other arithmetic  88.3 us (18%)
  between operations  14.8 us (3%)
  matrix products  12.9 us (3%)
  local copies, waits for them, and re-layouts  11 us (2%)
  starting transfers between devices  10.4 us (2%)
    psum x1, waiting for transfers between devices, local(): gram_sum = lax.psum(product, ('aa', 'ba'))  247 us
    unnamed x3, waiting for transfers between devices  80.2 us
    another operation x4, other arithmetic, local(): lower_factor = jnp.linalg.cholesky(gram_sum)  47.1 us
    another operation x2, other arithmetic, local(): lax.linalg.triangular_solve(lower_factor, identity, left_side=True, lower...  39.4 us
    all_to_all x1, waiting for transfers between devices, local(): lax.all_to_all(block_spec, 'aa', split_axis=3, concat_axis=0, tiled=True)  14.8 us
    all_to_all x1, starting transfers between devices, local(): lax.all_to_all(block_spec, 'aa', split_axis=3, concat_axis=0, tiled=True)  10.1 us
  transfers between devices with their start and end apart: 3, of which 3 were waited for; matrix products, arithmetic and copies ran while one was open for 0% of the time, Pallas kernels for 0%

commit v1 on v0

--- a/solution.py
+++ b/solution.py
@@ -41,7 +41,8 @@
         FREQS, columns, pts_dev
     )
     product = jnp.einsum("fip,fjp->fij", cols, cols, precision=lax.Precision.HIGHEST)
-    gram_sum = lax.psum(product, ("aa", "ba"))
+    partial_2 = lax.psum(product, "aa")
+    gram_sum = lax.psum(partial_2, "ba")
     lower_factor = jnp.linalg.cholesky(gram_sum)
     identity = jnp.broadcast_to(jnp.eye(columns, dtype=gram_sum.dtype), lower_factor.shape)
     inverse = lax.linalg.triangular_solve(lower_factor, identity, left_side=True, lower=True)

time: 479 us -> 436 us (0.910)
  waiting for transfers between devices: 342 us -> 285 us
  blocking collectives: 0 us -> 25 us
  starting transfers between devices: 10.4 us -> 0.3 us
    psum x1 -> x2, waiting for transfers between devices: 247 us -> 205 us  [the longest x1 139 us: local(): partial_2 = lax.psum(product, 'aa')]
    all_to_all x0 -> x1, blocking collectives: none -> 25 us  [local(): lax.all_to_all(block_spec, 'aa', split_axis=3, concat_axis=0, tiled=True)]
    all_to_all x1 -> x0, waiting for transfers between devices: 14.8 us -> none  [local(): lax.all_to_all(block_spec, 'aa', split_axis=3, concat_axis=0, tiled=True)]
    all_to_all x1 -> x0, starting transfers between devices: 10.1 us -> none  [local(): lax.all_to_all(block_spec, 'aa', split_axis=3, concat_axis=0, tiled=True)]
    unnamed x3 -> x4, waiting for transfers between devices: 80.2 us -> 80.1 us
where the time goes in v1:
time: 436 us
  waiting for transfers between devices  285 us (65%)
  other arithmetic  88.3 us (20%)
  blocking collectives  25 us (6%)
  between operations  14.5 us (3%)
  matrix products  12.9 us (3%)
  local copies, waits for them, and re-layouts  10.2 us (2%)
    psum x1, waiting for transfers between devices, local(): partial_2 = lax.psum(product, 'aa')  139 us
    unnamed x4, waiting for transfers between devices  80.1 us
    psum x1, waiting for transfers between devices, local(): gram_sum = lax.psum(partial_2, 'ba')  65.4 us
    another operation x4, other arithmetic, local(): lower_factor = jnp.linalg.cholesky(gram_sum)  47.1 us
    another operation x2, other arithmetic, local(): lax.linalg.triangular_solve(lower_factor, identity, left_side=True, lower...  39.4 us
    all_to_all x1, blocking collectives, local(): lax.all_to_all(block_spec, 'aa', split_axis=3, concat_axis=0, tiled=True)  25 us
    dot_general x1, matrix products, local(): jnp.einsum('savq,sgf->vgfaq', arranged, table, precision=lax.Precision.HI...  9.16 us
    unnamed x6, local copies, waits for them, and re-layouts  9.1 us
  transfers between devices with their start and end apart: 3, of which 3 were waited for; matrix products, arithmetic and copies ran while one was open for 0% of the time, Pallas kernels for 0%

profile of v1, /device:TPU:2, one launch (start us, length us, event | category | flops | bytes accessed | tf_op | source)
XLA Modules:
  0.0 435.9 jit_solution(16151034163997829041)
XLA Ops:
  7.2 0.0 all-reduce.9.cloned.1.call-start
  7.3 0.6 multiply_reduce_fusion
  8.6 5.9 %copy.38 = f32[4,8,256,256]{3,2,1,0:T(8,128)S(1)} copy(f32[4,8,256,256]{3,1,2,0:T(8,128)} %bitcast.42) | data formatting | bytes 16777216
  14.6 0.1 multiply_multiply_fusion.1
  14.7 0.0 copy-start
  14.7 9.2 %fusion.3 = f32[8,2,8,32,256]{4,2,0,3,1:T(8,128)} fusion(f32[32,32,8,256]{3,2,1,0:T(8,128)S(1)} %bitcast.41, f32[32,1,8]{0,2,1:T(8,128)S(1)} %get-tuple-element.13, f32[32,1,8]{0,2,1:T(8,128)S(1)} %get-tuple-element.12), kind=kOutput, calls=%fused_computation.3 | convolution fusion | flops 402653696 | bytes 12584960 | tf_op jit(solution)/shard_map/savq,sgf->vgfaq/dot_general | solution.py:35
  23.9 0.0 all-reduce.9.cloned.1.call-update
  23.9 0.0 all-reduce.5.cloned.1.call-start
  23.9 0.0 copy-done
  24.0 0.6 dynamic-slice
  24.5 80.1 %all-reduce.9.cloned.1.call-done = f32[8,2,8,32,256]{4,2,0,3,1:T(8,128)} async-done(((f32[8,2,8,32,256]{4,2,0,3,1:T(8,128)}), f32[8,2,8,32,256]{4,2,0,3,1:T(8,128)}) %all-reduce.9.cloned.1.call-update) | async-done | bytes 4194320
  104.6 1.7 constant_dynamic-slice_fusion
  106.3 0.1 copy.25
  106.4 25.0 %all_to_all.15 = f32[1,2,8,32,256]{4,2,0,1,3:T(8,128)S(1)} all-to-all(f32[1,2,8,32,256]{4,2,0,1,3:T(8,128)S(1)} %copy.25), channel_id=1, replica_groups=mesh['aa'=32,'ba'=8] {'aa'}, dimensions={3} | all-to-all | bytes 1048576 | tf_op jit(solution)/shard_map/all_to_all | solution.py:37
  131.4 1.6 fusion.7
  133.0 0.0 all-reduce.5.cloned.1.call-update
  133.0 0.2 all-reduce.7.cloned.1.call-start
  133.3 139.1 %all-reduce.5.cloned.1.call-done = f32[8,64,64]{1,2,0:T(8,128)} async-done(((f32[8,64,64]{1,2,0:T(8,128)}), f32[8,64,64]{1,2,0:T(8,128)}) %all-reduce.5.cloned.1.call-update) | async-done | bytes 131088 | tf_op jit(solution)/shard_map/psum | solution.py:44
  272.4 0.0 all-reduce.7.cloned.1.call-update
  272.4 65.4 %all-reduce.7.cloned.1.call-done = f32[8,64,64]{1,2,0:T(8,128)} async-done(((f32[8,64,64]{1,2,0:T(8,128)}), f32[8,64,64]{1,2,0:T(8,128)}) %all-reduce.7.cloned.1.call-update) | async-done | bytes 131088 | tf_op jit(solution)/shard_map/psum | solution.py:45
  337.8 1.1 copy.29
  338.9 1.0 fusion.11
  339.9 46.9 %custom-call.7 = f32[8,64,64]{2,1,0:T(8,128)S(1)} custom-call(f32[8,64,64]{2,1,0:T(8,128)S(1)} %fusion.11), custom_call_target="Cholesky" | custom-call | tf_op jit(solution)/shard_map/jit(cholesky)/cholesky | solution.py:46
  386.9 0.1 compare_reduce_fusion
  387.0 0.1 select_bitcast_fusion
  387.1 39.3 %custom-call.8 = f32[8,1,64,64]{2,3,1,0:T(8,128)S(1)} custom-call(f32[8,1,64,64]{3,2,1,0:T(8,128)S(1)} %get-tuple-element.10), custom_call_target="InvertDiagBlocksLowerTriangular" | custom-call | tf_op jit(solution)/shard_map/triangular_solve | solution.py:48
  426.4 0.6 fusion.9
  427.0 1.5 convolution_multiply_fusion
  428.6 0.8 copy.32
  (7 shorter events, 0.1 us)
Async XLA Ops:
  7.2 97.5 %all-reduce.9.cloned.1.call-start = ((), (), s32[]{:S(2)}) async-start(), calls=%async_computation.3 | async-start | bytes 8388608
  14.7 9.3 %copy-start = (u32[256]{0:T(256)S(1)}, u32[256]{0:T(256)}, u32[]{:S(2)}) copy-start(u32[256]{0:T(256)} %constant.81) | copy-start | bytes 3076
  23.9 248.5 %all-reduce.5.cloned.1.call-start = ((), (), s32[]{:S(2)}) async-start(), calls=%async_computation.1 | async-start | bytes 524288 | tf_op jit(solution)/shard_map/psum | solution.py:44
  133.0 204.8 %all-reduce.7.cloned.1.call-start = ((), (), s32[]{:S(2)}) async-start(), calls=%async_computation.2 | async-start | bytes 524288 | tf_op jit(solution)/shard_map/psum | solution.py:45
Sparse Core Ops, SparseCore 0:
  24.0 80.5 all-reduce.8
  133.1 139.1 all-reduce.4
  274.7 63.1 all-reduce.6
